TPU v7x, 128 devices: a whole 4x4x4 slice. The times are simulated.
128 devices in a mesh: seq: 16 (over x, y), exp: 8 (over z, core).
Axes of the slice: x: 4, y: 4, z: 4, core: 2. Of those that a mesh axis runs over, the one named last changes fastest.
Arguments:
- hidden: bfloat16 [2048, 4096], P('seq', 'exp'), may hold values from -6 to 6
- queries: bfloat16 [2048, 4096], P('seq', 'exp'), may hold values from -40 to 40
- keys: bfloat16 [2048, 1024], P('seq', 'exp'), may hold values from -6 to 6
- values: bfloat16 [2048, 1024], P('seq', 'exp'), may hold values from -6 to 6
- block_place: int32 [32], replicated, may hold values from 0 to 31, as said below
- page_table: int32 [128], replicated, may hold values from 0 to 127, each once
- out_weight: bfloat16 [4096, 4096], P('exp'), may hold values from -0.09375 to 0.09375
- norm_gain: float32 [4096], replicated, may hold values from 0.5 to 2
- gate_probs: float32 [2048, 2], P('seq'), may hold values from 0.1 to 1
- routes: int32 [2048, 2], P('seq'), may hold values from 0 to 7, all different within a row; in each aligned block of 128 rows (0 to 127, 128 to 255, ...) at most 64 rows name the same one
- w_gate: bfloat16 [8, 4096, 14336], P('exp', None, 'seq'), may hold values from -0.09375 to 0.09375
- w_up: bfloat16 [8, 4096, 14336], P('exp', None, 'seq'), may hold values from -0.09375 to 0.09375
- w_down: bfloat16 [8, 14336, 4096], P('exp', 'seq'), may hold values from -0.046875 to 0.046875
Outputs:
- layer_out: bfloat16 [2048, 4096], P('seq', 'exp')
- key_value_pages: bfloat16 [128, 16, 2, 1024], P('seq', None, None, 'exp')
Inputs may be any that keep to these rules, and one draw needn't show every extreme that they name: `block_place`: the first 24 entries are a permutation of 0 to 23, the others a permutation of 24 to 31. `page_table`: A permutation of the pages. `routes`: in the rows of one index of seq (128 rows) no expert is named more than 64 times, a bound that some block reaches; a row names two different experts.
All inputs are finite; a program needn't handle non-finite values.
Results may differ from a plain program's by a relative error of at most 0.02.
Values may be sent and summed in bfloat16 or wider, within the bound.
No kernel may reach another device: no remote copies, remote signals or barrier semaphores. Data moves between devices by JAX's collectives and lax.ppermute only.
A program may use at most 128 MiB of HBM per device.

v0:
```python
import math

import jax
import jax.numpy as jnp
from jax import lax
from jax.sharding import PartitionSpec as P

HEAD_SIZE = 128
NEXP = 8
PAGE_TOKENS = 16


THETA = 1000000.0
EPS = 1e-05


def apply_rotary(values_in, positions, head_count):
    row_count = values_in.shape[0]
    split_view = values_in.astype(jnp.float32).reshape(row_count, head_count, HEAD_SIZE)
    steps_half = jnp.arange(HEAD_SIZE // 2, dtype=jnp.float32)
    frequency = THETA ** (-(2.0 * steps_half) / HEAD_SIZE)
    angles = positions.astype(jnp.float32)[:, None] * frequency[None, :]
    cosine = jnp.cos(angles)[:, None, :]
    sine_part = jnp.sin(angles)[:, None, :]
    front_half = split_view[..., : HEAD_SIZE // 2]
    back_half = split_view[..., HEAD_SIZE // 2 :]
    turned = jnp.concatenate(
        [front_half * cosine - back_half * sine_part, back_half * cosine + front_half * sine_part],
        axis=-1,
    )
    return turned.reshape(row_count, head_count * HEAD_SIZE).astype(jnp.bfloat16)


def per_device(
    hidden,
    queries,
    keys,
    values,
    block_place,
    page_table,
    out_weight,
    norm_gain,
    gate_probs,
    routes,
    w_gate,
    w_up,
    w_down,
):
    seq_count = lax.axis_size("seq")
    exp_count = lax.axis_size("exp")
    seq_index = lax.axis_index("seq")
    tok_rows = queries.shape[0]
    half_rows = tok_rows // 2
    all_rows = tok_rows * seq_count
    long_len = 3 * all_rows // 4
    every_row = jnp.arange(all_rows, dtype=jnp.int32)
    all_pos = block_place[every_row // half_rows] * half_rows + every_row % half_rows
    my_pos = lax.dynamic_slice_in_dim(all_pos, seq_index * tok_rows, tok_rows)
    my_long = my_pos >= long_len
    my_rope = my_pos - long_len * my_long.astype(jnp.int32)
    q_heads = queries.shape[1] // HEAD_SIZE
    kv_heads = keys.shape[1] // HEAD_SIZE
    query_head_group = q_heads // kv_heads
    query_rotated = apply_rotary(queries, my_rope, q_heads)
    key_rotated = apply_rotary(keys, my_rope, kv_heads)
    q_grid = query_rotated.reshape(tok_rows, kv_heads, query_head_group, HEAD_SIZE)
    score_scale = 1.0 / math.sqrt(HEAD_SIZE)
    page_count = tok_rows // PAGE_TOKENS
    inverse_table = jnp.argsort(page_table)
    my_logical = lax.dynamic_slice_in_dim(inverse_table, seq_index * page_count, page_count)
    row_at = jnp.argsort(all_pos)
    taken = row_at[
        (
            my_logical[:, None] * PAGE_TOKENS + jnp.arange(PAGE_TOKENS, dtype=jnp.int32)[None, :]
        ).reshape(page_count * PAGE_TOKENS)
    ]
    key_all, value_all = (
        lax.all_gather(key_rotated, "seq", axis=0, tiled=True),
        lax.all_gather(values, "seq", axis=0, tiled=True),
    )
    peak_old = jnp.full((kv_heads, query_head_group, tok_rows), -1e30, jnp.float32)
    row_count = key_all.shape[0]
    scores = (
        jnp.einsum(
            "tkgd,nkd->kgtn",
            q_grid,
            key_all.reshape(row_count, kv_heads, HEAD_SIZE),
            preferred_element_type=jnp.float32,
        )
        * score_scale
    )
    allowed = ((all_pos >= long_len)[None, :] == my_long[:, None]) & (
        all_pos[None, :] <= my_pos[:, None]
    )
    scores = jnp.where(allowed, scores, -1e30)
    peak_new = jnp.maximum(peak_old, jnp.max(scores, axis=-1))
    weights = jnp.where(allowed, jnp.exp(scores - peak_new[..., None]), 0.0)
    total_new = jnp.sum(weights, axis=-1)
    summed = jnp.einsum(
        "kgtn,nkd->kgtd",
        weights.astype(jnp.bfloat16),
        value_all.reshape(row_count, kv_heads, HEAD_SIZE),
        preferred_element_type=jnp.float32,
    )
    peak_final, total_final, summed = (peak_new, total_new, summed)
    cache_pages = jnp.stack([key_all[taken], value_all[taken]], axis=1).reshape(
        page_count, PAGE_TOKENS, 2, kv_heads * HEAD_SIZE
    )
    attended = (
        (summed / total_final[..., None])
        .transpose(2, 0, 1, 3)
        .reshape(tok_rows, q_heads * HEAD_SIZE)
        .astype(jnp.bfloat16)
    )
    partial_proj = jnp.dot(attended, out_weight, preferred_element_type=jnp.float32)
    projected = lax.psum_scatter(
        partial_proj.astype(jnp.bfloat16), "exp", scatter_dimension=1, tiled=True
    ).astype(jnp.float32)
    residual = (hidden.astype(jnp.float32) + projected).astype(jnp.bfloat16)
    top_count = routes.shape[1]
    capacity = tok_rows // 2
    assign_count = tok_rows * top_count
    flat_routes = routes.reshape(assign_count)
    expert_hot = (flat_routes[:, None] == jnp.arange(NEXP, dtype=jnp.int32)[None, :]).astype(
        jnp.float32
    )
    earlier = (jnp.arange(assign_count)[:, None] > jnp.arange(assign_count)[None, :]).astype(
        jnp.float32
    )
    before = jnp.dot(earlier, expert_hot, preferred_element_type=jnp.float32)
    slot_rank = jnp.sum(before * expert_hot, axis=1).astype(jnp.int32).reshape(tok_rows, top_count)
    slot_grid = routes * capacity + slot_rank
    chooser = jnp.any(
        slot_grid[None, :, :] == jnp.arange(NEXP * capacity, dtype=jnp.int32)[:, None, None],
        axis=-1,
    ).astype(jnp.bfloat16)
    outgoing_rows = jnp.dot(chooser, residual, preferred_element_type=jnp.float32).astype(
        jnp.bfloat16
    )
    expert_local = NEXP // exp_count
    arrived_rows = lax.all_to_all(
        outgoing_rows.reshape(exp_count, expert_local * capacity, -1),
        "exp",
        split_axis=0,
        concat_axis=2,
        tiled=True,
    )
    gathered_in = arrived_rows.astype(jnp.float32)
    mean_square = jnp.mean(gathered_in * gathered_in, axis=-1, keepdims=True)
    normed = (gathered_in * lax.rsqrt(mean_square + EPS) * norm_gain).astype(jnp.bfloat16)
    token_rows = lax.all_gather(normed, "seq", axis=1, tiled=True)
    gate_part = jnp.einsum("end,edf->enf", token_rows, w_gate, preferred_element_type=jnp.float32)
    up_part = jnp.einsum("end,edf->enf", token_rows, w_up, preferred_element_type=jnp.float32)
    hidden_units = (jax.nn.silu(gate_part) * up_part).astype(jnp.bfloat16)
    returned = lax.psum_scatter(
        jnp.einsum("enf,efd->ned", hidden_units, w_down, preferred_element_type=jnp.float32).astype(
            jnp.bfloat16
        ),
        "seq",
        scatter_dimension=0,
        tiled=True,
    )
    homed = lax.all_to_all(returned, "exp", split_axis=2, concat_axis=1, tiled=True)
    lookup = homed.reshape(capacity * NEXP, -1)
    chosen = (
        lookup[(slot_rank * NEXP + routes).reshape(assign_count)]
        .astype(jnp.float32)
        .reshape(tok_rows, top_count, -1)
    )
    gate_share = gate_probs / jnp.sum(gate_probs, axis=1, keepdims=True)
    layer_out = (
        residual.astype(jnp.float32) + jnp.sum(gate_share[:, :, None] * chosen, axis=1)
    ).astype(jnp.bfloat16)
    return (layer_out, cache_pages)


def solution(mesh):
    return jax.shard_map(
        per_device,
        mesh=mesh,
        in_specs=(
            P("seq", "exp"),
            P("seq", "exp"),
            P("seq", "exp"),
            P("seq", "exp"),
            P(),
            P(),
            P("exp", None),
            P(),
            P("seq", None),
            P("seq", None),
            P("exp", None, "seq"),
            P("exp", None, "seq"),
            P("exp", "seq", None),
        ),
        out_specs=(P("seq", "exp"), P("seq", None, None, "exp")),
        check_vma=False,
    )
```

profile of v0, /device:TPU:1, one launch (start us, length us, event | category | flops | bytes accessed | tf_op | source)
XLA Modules:
  0.0 390.9 jit_solution(8095771630104824144)
XLA Ops:
  8.4 1.8 fusion.55
  10.2 2.1 fusion.54
  12.3 4.3 %compare_select_fusion.1 = s32[2048,1]{0,1:T(1,128)S(1)} fusion(s32[]{:T(128)} %bitcast.25, s32[]{:T(128)} %bitcast.26, s32[]{:T(128)} %bitcast.27, s32[]{:T(128)} %bitcast.28, s32[]{:T(128)} %bitcast.29, s32[]{:T(128)} %bitcast.31, s32[]{:T(128)} %bitcast.30), kind=kLoop, calls=%fused_computation.88 | loop fusion | flops 47104 | bytes 8220 | tf_op jit(solution)/shard_map/gather | solution.py:57
  16.7 15.8 %broadcast_compare_fusion = (pred[2048]{0:T(1024)(128)(4,1)S(1)}, s32[2048]{0:T(1024)S(1)}) fusion(pred[2048]{0:T(1024)(128)(4,1)S(1)} %compare_reduce_fusion, pred[2048]{0:T(1024)(128)(4,1)S(1)} %compare_reduce_fusion.1, pred[2048]{0:T(1024)(128)(4,1)S(1)} %compare_reduce_fusion.2, pred[2048]{0:T(1024)(128)(4,1)S(1)} %compare_reduce_fusion.3, ...), kind=kLoop, calls=%fused_computation.112 | loop fusion | flops 69632 | bytes 69732 | tf_op jit(solution)/shard_map/ge | solution.py:92
  32.4 0.1 broadcast_compare_fusion.1
  32.5 0.9 copy.61
  33.4 0.3 multiply_cosine_fusion
  33.7 0.2 fusion.38
  33.9 1.0 copy.62
  35.0 0.1 copy.78
  35.1 0.1 copy.77
  35.3 20.5 %all-gather = bf16[2048,1,128]{0,2,1:T(8,128)(2,1)S(1)} all-gather(bf16[128,1,128]{0,2,1:T(8,128)(2,1)S(1)} %pad_maximum_fusion.1), channel_id=2, replica_groups=mesh['seq'=16,'exp'=8] {'seq'}, dimensions={0}, use_global_device_ids=true | all-gather | bytes 557056 | tf_op jit(solution)/shard_map/all_gather | solution.py:78
  55.8 18.2 %all_gather.10 = bf16[2048,128]{1,0:T(8,128)(2,1)S(1)} all-gather(bf16[128,128]{1,0:T(8,128)(2,1)} %param.16), channel_id=1, replica_groups=mesh['seq'=16,'exp'=8] {'seq'}, dimensions={0}, use_global_device_ids=true | all-gather | bytes 557056 | tf_op jit(solution)/shard_map/all_gather | solution.py:79
  74.0 1.5 compare_and_fusion
  75.5 0.1 subtract_convert_fusion
  75.6 0.8 fusion.7
  76.5 1.0 fusion.8
  77.5 1.1 fusion.22
  78.6 1.1 copy-done
  79.7 1.7 convolution_convert_fusion
  81.5 0.1 copy.67
  81.6 0.1 eq.46
  81.8 0.2 fusion.18
  82.0 0.1 convert_element_type.133
  82.2 0.1 fusion.29
  82.3 39.0 %reduce-scatter.3.cloned.1.call-done = bf16[128,512]{1,0:T(8,128)(2,1)} async-done(((bf16[128,4096]{1,0:T(8,128)(2,1)}), bf16[128,512]{1,0:T(8,128)(2,1)}) %reduce-scatter.3.cloned.1.call-update) | async-done | bytes 131088 | tf_op jit(solution)/shard_map/reduce_scatter | solution.py:116
  121.3 1.2 convolution_convert_fusion.1
  122.5 15.3 %all_to_all.8 = bf16[8,64,512]{2,1,0:T(8,128)(2,1)S(1)} all-to-all(bf16[8,64,512]{2,1,0:T(8,128)(2,1)S(1)} %bitcast.130), channel_id=1, replica_groups=mesh['seq'=16,'exp'=8] {'exp'}, dimensions={0} | all-to-all | bytes 1048576 | tf_op jit(solution)/shard_map/all_to_all | solution.py:141
  137.8 0.2 fusion.25
  138.0 0.1 convert_bitcast_fusion.1
  138.1 0.1 copy.79
  138.3 1.0 multiply_convert_fusion.1
  139.3 0.2 reduce-scatter.5.cloned.1.call-start
  139.5 70.0 %all-gather.3.cloned.1.call-done = bf16[1,1024,4096]{2,1,0:T(8,128)(2,1)} async-done(((bf16[1,64,4096]{2,1,0:T(8,128)(2,1)}), bf16[1,1024,4096]{2,1,0:T(8,128)(2,1)}) %all-gather.3.cloned.1.call-update) | async-done | bytes 8388624 | tf_op jit(solution)/shard_map/all_gather | solution.py:151
  209.5 12.5 %fusion = f32[1024,896]{1,0:T(8,128)S(1)} fusion(bf16[1,1024,4096]{2,1,0:T(8,128)(2,1)} %all-gather.3.cloned.1.call-done, bf16[1,4096,896]{2,1,0:T(8,128)(2,1)} %param.24), kind=kOutput, calls=%fused_computation.4 | convolution fusion | flops 7516192768 | bytes 19398656 | tf_op jit(solution)/shard_map/end,edf->enf/dot_general | solution.py:153
  222.0 12.1 %multiply_convert_fusion = bf16[1024,896]{1,0:T(8,128)(2,1)S(1)} fusion(f32[1024,896]{1,0:T(8,128)S(1)} %fusion, bf16[1,4096,896]{2,1,0:T(8,128)(2,1)} %param.23, bf16[1,1024,4096]{2,1,0:T(8,128)(2,1)S(1)} %copy-done.6), kind=kOutput, calls=%fused_computation.16 | convolution fusion | flops 7521697792 | bytes 21233664 | tf_op jit(solution)/shard_map/end,edf->enf/dot_general | solution.py:152
  234.1 11.1 %convert_bitcast_fusion = bf16[1024,1,4096]{2,0,1:T(8,128)(2,1)} fusion(bf16[1024,896]{1,0:T(8,128)(2,1)S(1)} %multiply_convert_fusion, bf16[1,896,4096]{2,1,0:T(8,128)(2,1)S(1)} %bitcast.138), kind=kOutput, calls=%fused_computation.8 | convolution fusion | flops 7520387072 | bytes 17563648 | tf_op jit(solution)/shard_map/enf,efd->ned/dot_general | solution.py:156
  245.2 0.6 copy-done.7
  245.9 2.5 sort.35
  248.4 0.1 dynamic-slice_multiply_fusion
  248.5 0.1 iota_add_fusion
  248.5 0.1 add.166
  248.6 5.0 %sort.34 = (s32[2048]{0:T(1024)}, s32[2048]{0:T(1024)S(1)}) sort(s32[2048]{0:T(1024)S(1)} %get-tuple-element.7, s32[2048]{0:T(1024)S(1)} %iota.49), dimensions={0}, to_apply=%region_9.10 | sort | flops 22528 | bytes 32768 | tf_op jit(solution)/shard_map/jit(argsort)/sort | solution.py:71
  253.7 1.1 gather_fusion.1
  254.9 74.9 %reduce-scatter.5.cloned.1.call-done = bf16[64,1,4096]{2,0,1:T(8,128)(2,1)} async-done(((bf16[1024,1,4096]{2,0,1:T(8,128)(2,1)}), bf16[64,1,4096]{2,0,1:T(8,128)(2,1)}) %reduce-scatter.5.cloned.1.call-update) | async-done | bytes 524304 | tf_op jit(solution)/shard_map/reduce_scatter | solution.py:155
  329.8 4.9 %copy.70 = bf16[64,1,4096]{0,1,2:T(2,128)(2,1)S(1)} copy(bf16[64,1,4096]{2,0,1:T(8,128)(2,1)} %reduce-scatter.5.cloned.1.call-done) | data formatting | bytes 1048576 | tf_op jit(solution)/shard_map/reduce_scatter | solution.py:155
  334.7 0.5 broadcast.624
  335.2 23.6 %reduce.56 = bf16[4096,64]{1,0:T(8,128)(2,1)} reduce(bf16[4096,1,64]{2,1,0:T(2,128)(2,1)S(1)} %bitcast.127, bf16[]{:T(256)} %broadcast.624), dimensions={1}, to_apply=%bitcast.118.reduce_sub_computation | reduce | bytes 1048578
  358.8 3.0 reshape.625
  361.8 6.6 %all-to-all-start.1 = ((bf16[8,2,16384]{2,1,0:T(2,128)(2,1)}), bf16[8,2,16384]{2,1,0:T(2,128)(2,1)S(1)}, u32[]{:S(2)}, u32[]{:S(2)}) async-start(bf16[8,2,16384]{2,1,0:T(2,128)(2,1)} %reshape.625), calls=%async_computation.3 | async-start | bytes 1048576 | tf_op jit(solution)/shard_map/all_to_all | solution.py:163
  368.4 0.1 copy.66
  368.5 0.1 reshape.441
  368.6 0.7 gather_fusion.3
  369.4 0.3 copy.73
  369.7 0.7 gather_fusion.2
  370.5 0.8 pad_maximum_fusion
  371.3 6.5 %all-to-all-done.1 = bf16[8,2,16384]{2,1,0:T(2,128)(2,1)S(1)} async-done(((bf16[8,2,16384]{2,1,0:T(2,128)(2,1)}), bf16[8,2,16384]{2,1,0:T(2,128)(2,1)S(1)}, u32[]{:S(2)}, u32[]{:S(2)}) %all-to-all-start.1) | async-done | bytes 524320 | tf_op jit(solution)/shard_map/all_to_all | solution.py:163
  377.7 1.2 reshape.626
  379.0 2.3 copy.71
  381.2 0.2 reshape.440
  381.5 1.2 gather_fusion
  382.6 0.3 reshape.447
  383.0 0.7 multiply_reduce_fusion
  383.7 0.7 add_convert_fusion
  (72 shorter events, 1.6 us)
Async XLA Ops:
  7.2 114.1 %reduce-scatter.3.cloned.1.call-start = ((), (), s32[]{:S(2)}) async-start(), calls=%async_computation.4 | async-start | bytes 1179648 | tf_op jit(solution)/shard_map/reduce_scatter | solution.py:116
  77.5 2.2 copy-start
  78.6 2.9 copy-start.4
  78.6 42.7 %copy-start.1 = (bf16[128,512]{1,0:T(8,128)(2,1)S(1)}, bf16[128,512]{1,0:T(8,128)(2,1)}, u32[]{:S(2)}) copy-start(bf16[128,512]{1,0:T(8,128)(2,1)} %param.13) | copy-start | bytes 393220
  81.4 56.8 %copy-start.3 = (f32[4096]{0:T(1024)S(1)}, f32[4096]{0:T(1024)}, u32[]{:S(2)}) copy-start(f32[4096]{0:T(1024)} %param.20) | copy-start | bytes 49156
  81.4 128.1 %all-gather.3.cloned.1.call-start = ((), (), s32[]{:S(2)}) async-start(), calls=%async_computation.5 | async-start | bytes 8912896 | tf_op jit(solution)/shard_map/all_gather | solution.py:151
  139.3 190.5 %reduce-scatter.5.cloned.1.call-start = ((), (), s32[]{:S(2)}) async-start(), calls=%async_computation.6 | async-start | bytes 8912896 | tf_op jit(solution)/shard_map/reduce_scatter | solution.py:155
  209.5 12.5 %copy-start.6 = (bf16[1,1024,4096]{2,1,0:T(8,128)(2,1)S(1)}, bf16[1,1024,4096]{2,1,0:T(8,128)(2,1)}, u32[]{:S(2)}) copy-start(bf16[1,1024,4096]{2,1,0:T(8,128)(2,1)} %all-gather.3.cloned.1.call-done) | copy-start | bytes 25165828
  209.5 24.6 %slice-start = ((s8[7340032]{0:T(1024)(128)(4,1)}), s8[4194304]{0:T(1024)(128)(4,1)S(1)}, s32[]{:S(2)}) async-start(s8[7340032]{0:T(1024)(128)(4,1)} %bitcast.137), calls=%async_computation.7 | async-start | bytes 8388608
  222.0 12.1 %slice-start.1 = ((s8[7340032]{0:T(1024)(128)(4,1)}), s8[3145728]{0:T(1024)(128)(4,1)S(1)}, s32[]{:S(2)}) async-start(s8[7340032]{0:T(1024)(128)(4,1)} %bitcast.137), calls=%async_computation.8 | async-start | bytes 6291456
  245.2 0.7 copy-start.7
  245.2 8.5 %copy-start.5 = (f32[128,2]{0,1:T(2,128)S(1)}, f32[128,2]{0,1:T(2,128)}, u32[]{:S(2)}) copy-start(f32[128,2]{0,1:T(2,128)} %param.21) | copy-start | bytes 3076
  361.8 15.9 %all-to-all-start.1 = ((bf16[8,2,16384]{2,1,0:T(2,128)(2,1)}), bf16[8,2,16384]{2,1,0:T(2,128)(2,1)S(1)}, u32[]{:S(2)}, u32[]{:S(2)}) async-start(bf16[8,2,16384]{2,1,0:T(2,128)(2,1)} %reshape.625), calls=%async_computation.3 | async-start | bytes 1048576 | tf_op jit(solution)/shard_map/all_to_all | solution.py:163
  379.0 4.7 %copy-start.2 = (bf16[128,512]{1,0:T(8,128)(2,1)S(1)}, bf16[128,512]{1,0:T(8,128)(2,1)}, u32[]{:S(2)}) copy-start(bf16[128,512]{1,0:T(8,128)(2,1)} %reduce-scatter.3.cloned.1.call-done) | copy-start | bytes 393220
Sparse Core Ops, SparseCore 0:
  81.6 39.6 reduce-scatter.2
  139.4 70.0 all-gather.2
  245.4 84.3 reduce-scatter.4
where the time goes:
time: 392 us; the launch traced here: 391 us
  waiting for transfers between devices  190 us (48%)
  other arithmetic  59.5 us (15%)
  blocking collectives  54.1 us (14%)
  matrix products  40.6 us (10%)
  local copies, waits for them, and re-layouts  25.3 us (6%)
  between operations  14.2 us (4%)
  starting transfers between devices  6.86 us (2%)
    reduce_scatter x1, waiting for transfers between devices, per_device(): lax.psum_scatter(jnp.einsum('enf,efd->ned', hidden_units, w_down, preferr...  74.9 us
    all_gather x1, waiting for transfers between devices, per_device(): token_rows = lax.all_gather(normed, 'seq', axis=1, tiled=True)  70 us
    reduce_scatter x1, waiting for transfers between devices, per_device(): lax.psum_scatter(partial_proj.astype(jnp.bfloat16), 'exp', scatter_dimens...  39 us
    unnamed x3, other arithmetic  23.7 us
    all_gather x1, blocking collectives, per_device(): lax.all_gather(key_rotated, 'seq', axis=0, tiled=True)  20.5 us
    all_gather x1, blocking collectives, per_device(): lax.all_gather(values, 'seq', axis=0, tiled=True)  18.2 us
    ge x1, other arithmetic, per_device(): all_pos >= long_len  15.8 us
    all_to_all x1, blocking collectives, per_device(): lax.all_to_all(outgoing_rows.reshape(exp_count, expert_local * capacity,...  15.3 us
  transfers between devices with their start and end apart: 4, of which 4 were waited for; matrix products, arithmetic and copies ran while one was open for 3% of the time, Pallas kernels for 0%

commit v1 on v0

--- a/solution.py
+++ b/solution.py
@@ -8,6 +8,7 @@
 HEAD_SIZE = 128
 NEXP = 8
 PAGE_TOKENS = 16
+CHUNKS = 2
 
 
 THETA = 1000000.0
@@ -53,8 +54,9 @@
     half_rows = tok_rows // 2
     all_rows = tok_rows * seq_count
     long_len = 3 * all_rows // 4
-    every_row = jnp.arange(all_rows, dtype=jnp.int32)
-    all_pos = block_place[every_row // half_rows] * half_rows + every_row % half_rows
+    all_pos = (
+        block_place[:, None] * half_rows + jnp.arange(half_rows, dtype=jnp.int32)[None, :]
+    ).reshape(all_rows)
     my_pos = lax.dynamic_slice_in_dim(all_pos, seq_index * tok_rows, tok_rows)
     my_long = my_pos >= long_len
     my_rope = my_pos - long_len * my_long.astype(jnp.int32)
@@ -66,18 +68,34 @@
     q_grid = query_rotated.reshape(tok_rows, kv_heads, query_head_group, HEAD_SIZE)
     score_scale = 1.0 / math.sqrt(HEAD_SIZE)
     page_count = tok_rows // PAGE_TOKENS
-    inverse_table = jnp.argsort(page_table)
-    my_logical = lax.dynamic_slice_in_dim(inverse_table, seq_index * page_count, page_count)
-    row_at = jnp.argsort(all_pos)
-    taken = row_at[
-        (
-            my_logical[:, None] * PAGE_TOKENS + jnp.arange(PAGE_TOKENS, dtype=jnp.int32)[None, :]
-        ).reshape(page_count * PAGE_TOKENS)
-    ]
-    key_all, value_all = (
-        lax.all_gather(key_rotated, "seq", axis=0, tiled=True),
-        lax.all_gather(values, "seq", axis=0, tiled=True),
-    )
+    page_total = page_table.shape[0]
+    my_pages = seq_index * page_count + jnp.arange(page_count, dtype=jnp.int32)
+    my_logical = jnp.sum(
+        jnp.where(
+            page_table[None, :] == my_pages[:, None],
+            jnp.arange(page_total, dtype=jnp.int32)[None, :],
+            0,
+        ),
+        axis=1,
+    )
+    block_count = block_place.shape[0]
+    slot_of_block = jnp.sum(
+        jnp.where(
+            block_place[None, :] == jnp.arange(block_count, dtype=jnp.int32)[:, None],
+            jnp.arange(block_count, dtype=jnp.int32)[None, :],
+            0,
+        ),
+        axis=1,
+    )
+    wanted_pos = (
+        my_logical[:, None] * PAGE_TOKENS + jnp.arange(PAGE_TOKENS, dtype=jnp.int32)[None, :]
+    ).reshape(page_count * PAGE_TOKENS)
+    taken = slot_of_block[wanted_pos // half_rows] * half_rows + wanted_pos % half_rows
+    kv_width = key_rotated.shape[1]
+    kv_all = lax.all_gather(
+        jnp.concatenate([key_rotated, values], axis=1), "seq", axis=0, tiled=True
+    )
+    key_all, value_all = kv_all[:, :kv_width], kv_all[:, kv_width:]
     peak_old = jnp.full((kv_heads, query_head_group, tok_rows), -1e30, jnp.float32)
     row_count = key_all.shape[0]
     scores = (
@@ -148,22 +166,35 @@
     gathered_in = arrived_rows.astype(jnp.float32)
     mean_square = jnp.mean(gathered_in * gathered_in, axis=-1, keepdims=True)
     normed = (gathered_in * lax.rsqrt(mean_square + EPS) * norm_gain).astype(jnp.bfloat16)
-    token_rows = lax.all_gather(normed, "seq", axis=1, tiled=True)
-    gate_part = jnp.einsum("end,edf->enf", token_rows, w_gate, preferred_element_type=jnp.float32)
-    up_part = jnp.einsum("end,edf->enf", token_rows, w_up, preferred_element_type=jnp.float32)
-    hidden_units = (jax.nn.silu(gate_part) * up_part).astype(jnp.bfloat16)
-    returned = lax.psum_scatter(
-        jnp.einsum("enf,efd->ned", hidden_units, w_down, preferred_element_type=jnp.float32).astype(
-            jnp.bfloat16
-        ),
-        "seq",
-        scatter_dimension=0,
-        tiled=True,
-    )
-    homed = lax.all_to_all(returned, "exp", split_axis=2, concat_axis=1, tiled=True)
-    lookup = homed.reshape(capacity * NEXP, -1)
+    chunk_count = CHUNKS
+    chunk_rows = capacity // chunk_count
+    pieces = []
+    for chunk in range(chunk_count):
+        token_rows = lax.all_gather(
+            normed[:, chunk * chunk_rows : (chunk + 1) * chunk_rows], "seq", axis=1, tiled=True
+        )
+        gate_part = jnp.einsum(
+            "end,edf->enf", token_rows, w_gate, preferred_element_type=jnp.float32
+        )
+        up_part = jnp.einsum("end,edf->enf", token_rows, w_up, preferred_element_type=jnp.float32)
+        hidden_units = (jax.nn.silu(gate_part) * up_part).astype(jnp.bfloat16)
+        pieces.append(
+            lax.psum_scatter(
+                jnp.einsum(
+                    "enf,efd->end", hidden_units, w_down, preferred_element_type=jnp.float32
+                ).astype(jnp.bfloat16),
+                "seq",
+                scatter_dimension=1,
+                tiled=True,
+            )
+        )
+    returned = jnp.concatenate(pieces, axis=1)
+    model_width = returned.shape[2]
+    outbound = returned.reshape(capacity, exp_count, model_width // exp_count).transpose(1, 0, 2)
+    homed = lax.all_to_all(outbound, "exp", split_axis=0, concat_axis=0, tiled=True)
+    lookup = homed.reshape(NEXP * capacity, -1)
     chosen = (
-        lookup[(slot_rank * NEXP + routes).reshape(assign_count)]
+        lookup[slot_grid.reshape(assign_count)]
         .astype(jnp.float32)
         .reshape(tok_rows, top_count, -1)
     )

time: 392 us -> 404 us (1.031)
  waiting for transfers between devices: 190 us -> 286 us
  other arithmetic: 59.5 us -> 8.93 us
  blocking collectives: 54.1 us -> 15.3 us
  matrix products: 40.6 us -> 59.5 us
  local copies, waits for them, and re-layouts: 25.3 us -> 12.4 us
    reduce_scatter x1 -> x2, waiting for transfers between devices: 74.9 us -> 131 us  [per_device(): lax.psum_scatter(jnp.einsum('enf,efd->end', hidden_units, w_down, preferr...]
    all_gather x1 -> x3, waiting for transfers between devices: 70 us -> 117 us  [the longest x2 76 us: per_device(): lax.all_gather(normed[:, chunk * chunk_rows:(chunk + 1) * chunk_rows], 's...]
    all_gather x2 -> x0, blocking collectives: 38.8 us -> none  [the longest x1 20.5 us: per_device(): lax.all_gather(key_rotated, 'seq', axis=0, tiled=True)]
    unnamed x3 -> x1, other arithmetic: 23.7 us -> 0.12 us
    ge x1, other arithmetic: 15.8 us -> 0.01 us  [per_device(): all_pos >= long_len]
    dot_general x2, matrix products: 23.6 us -> 33.2 us  [per_device(): jnp.einsum('enf,efd->end', hidden_units, w_down, preferred_element_type=j...]
    reduce_scatter x1, waiting for transfers between devices: 39 us -> 29.9 us  [per_device(): lax.psum_scatter(partial_proj.astype(jnp.bfloat16), 'exp', scatter_dimens...]
    dot_general x1 -> x2, matrix products: 12.1 us -> 20.1 us  [per_device(): jnp.einsum('end,edf->enf', token_rows, w_gate, preferred_element_type=jnp...]
  transfers between devices with their start and end apart: 4 -> 7, of which waited for: 4 -> 7; matrix products, arithmetic and copies ran while one was open for 3% -> 15% of each run, Pallas kernels for 0% -> 0%
where the time goes in v1:
time: 404 us
  waiting for transfers between devices  286 us (71%)
  matrix products  59.5 us (15%)
  blocking collectives  15.3 us (4%)
  between operations  14.5 us (4%)
  local copies, waits for them, and re-layouts  12.4 us (3%)
  other arithmetic  8.93 us (2%)
  starting transfers between devices  7.5 us (2%)
    reduce_scatter x2, waiting for transfers between devices, per_device(): lax.psum_scatter(jnp.einsum('enf,efd->end', hidden_units, w_down, preferr...  131 us
    all_gather x2, waiting for transfers between devices, per_device(): lax.all_gather(normed[:, chunk * chunk_rows:(chunk + 1) * chunk_rows], 's...  76 us
    all_gather x1, waiting for transfers between devices, per_device(): lax.all_gather(jnp.concatenate([key_rotated, values], axis=1), 'seq', axi...  41.5 us
    dot_general x2, matrix products, per_device(): jnp.einsum('enf,efd->end', hidden_units, w_down, preferred_element_type=j...  33.2 us
    reduce_scatter x1, waiting for transfers between devices, per_device(): lax.psum_scatter(partial_proj.astype(jnp.bfloat16), 'exp', scatter_dimens...  29.9 us
    dot_general x2, matrix products, per_device(): jnp.einsum('end,edf->enf', token_rows, w_gate, preferred_element_type=jnp...  20.1 us
    all_to_all x1, blocking collectives, per_device(): lax.all_to_all(outgoing_rows.reshape(exp_count, expert_local * capacity,...  15.3 us
  transfers between devices with their start and end apart: 7, of which 7 were waited for; matrix products, arithmetic and copies ran while one was open for 15% of the time, Pallas kernels for 0%

profile of v1, /device:TPU:1, one launch (start us, length us, event | category | flops | bytes accessed | tf_op | source)
XLA Modules:
  0.0 403.7 jit_solution(7229690235765857358)
XLA Ops:
  7.2 0.7 broadcast_multiply_fusion.1
  8.0 0.1 broadcast_compare_fusion.1
  8.1 0.9 copy.58
  9.0 0.9 copy.59
  9.9 0.2 fusion.71
  10.1 0.6 pad_maximum_fusion.1
  10.8 1.0 copy.60
  11.9 0.1 copy.75
  12.0 0.1 copy.76
  12.2 0.3 multiply_cosine_fusion
  12.5 0.1 subtract_convert_fusion
  12.6 1.5 compare_and_fusion
  14.1 41.5 %all-gather.4.cloned.1.call-done = bf16[2048,256]{0,1:T(8,128)(2,1)} async-done(((bf16[128,256]{0,1:T(8,128)(2,1)}), bf16[2048,256]{0,1:T(8,128)(2,1)}) %all-gather.4.cloned.1.call-update) | async-done | bytes 1048592 | tf_op jit(solution)/shard_map/all_gather | solution.py:95
  55.5 2.0 fusion.28
  57.5 1.0 fusion.29
  58.6 1.1 fusion.47
  59.7 1.1 copy-done
  60.7 1.7 convolution_convert_fusion
  62.6 0.1 copy.65
  62.7 0.1 eq.72
  62.8 0.2 fusion.43
  63.0 0.1 convert_element_type.137
  63.2 0.1 fusion.62
  63.3 29.9 %reduce-scatter.4.cloned.1.call-done = bf16[128,512]{1,0:T(8,128)(2,1)} async-done(((bf16[128,4096]{1,0:T(8,128)(2,1)}), bf16[128,512]{1,0:T(8,128)(2,1)}) %reduce-scatter.4.cloned.1.call-update) | async-done | bytes 131088 | tf_op jit(solution)/shard_map/reduce_scatter | solution.py:134
  93.3 1.2 convolution_convert_fusion.1
  94.5 15.3 %all_to_all.14 = bf16[8,64,512]{2,1,0:T(8,128)(2,1)S(1)} all-to-all(bf16[8,64,512]{2,1,0:T(8,128)(2,1)S(1)} %bitcast.130), channel_id=1, replica_groups=mesh['seq'=16,'exp'=8] {'exp'}, dimensions={0} | all-to-all | bytes 1048576 | tf_op jit(solution)/shard_map/all_to_all | solution.py:159
  109.8 0.1 convert_bitcast_fusion
  109.9 0.1 copy.77
  110.0 0.2 fusion.50
  110.2 0.2 multiply_convert_fusion.2
  110.4 0.9 fusion.87
  111.3 0.5 all-gather.8.cloned.1.call-update
  111.9 0.2 reduce-scatter.6.cloned.1.call-start
  112.1 50.0 %all-gather.6.cloned.1.call-done = bf16[1,512,4096]{2,1,0:T(8,128)(2,1)} async-done(((bf16[1,32,4096]{2,1,0:T(8,128)(2,1)}), bf16[1,512,4096]{2,1,0:T(8,128)(2,1)}) %all-gather.6.cloned.1.call-update) | async-done | bytes 4194320 | tf_op jit(solution)/shard_map/all_gather | solution.py:173
  162.1 10.1 %fusion.10 = f32[512,896]{1,0:T(8,128)S(1)} fusion(bf16[1,4096,896]{2,1,0:T(8,128)(2,1)} %param.23, bf16[1,512,4096]{2,1,0:T(8,128)(2,1)} %all-gather.6.cloned.1.call-done), kind=kOutput, calls=%fused_computation.14 | convolution fusion | flops 3758096384 | bytes 13369344 | tf_op jit(solution)/shard_map/end,edf->enf/dot_general | solution.py:176
  172.2 16.6 %fusion.21 = bf16[1,512,4096]{2,1,0:T(8,128)(2,1)} fusion(bf16[1,896,4096]{2,1,0:T(8,128)(2,1)} %param.25, f32[512,896]{1,0:T(8,128)S(1)} %fusion.10, bf16[1,4096,896]{2,1,0:T(8,128)(2,1)} %param.24, bf16[1,512,4096]{2,1,0:T(8,128)(2,1)} %all-gather.6.cloned.1.call-done), kind=kOutput, calls=%fused_computation.19 | convolution fusion | flops 7521042432 | bytes 24903680 | tf_op jit(solution)/shard_map/enf,efd->end/dot_general | solution.py:183
  188.8 0.3 reduce-scatter.8.cloned.1.call-start
  189.1 26.0 %all-gather.8.cloned.1.call-done = bf16[1,512,4096]{2,1,0:T(8,128)(2,1)} async-done(((bf16[1,32,4096]{2,1,0:T(8,128)(2,1)}), bf16[1,512,4096]{2,1,0:T(8,128)(2,1)}) %all-gather.8.cloned.1.call-update) | async-done | bytes 4194320 | tf_op jit(solution)/shard_map/all_gather | solution.py:173
  215.1 10.1 %fusion.8 = f32[512,896]{1,0:T(8,128)S(1)} fusion(bf16[1,4096,896]{2,1,0:T(8,128)(2,1)} %param.23, bf16[1,512,4096]{2,1,0:T(8,128)(2,1)} %all-gather.8.cloned.1.call-done), kind=kOutput, calls=%fused_computation.12 | convolution fusion | flops 3758096384 | bytes 13369344 | tf_op jit(solution)/shard_map/end,edf->enf/dot_general | solution.py:176
  225.2 16.5 %fusion.18 = bf16[1,512,4096]{2,1,0:T(8,128)(2,1)} fusion(bf16[1,896,4096]{2,1,0:T(8,128)(2,1)} %param.25, f32[512,896]{1,0:T(8,128)S(1)} %fusion.8, bf16[1,4096,896]{2,1,0:T(8,128)(2,1)} %param.24, bf16[1,512,4096]{2,1,0:T(8,128)(2,1)} %all-gather.8.cloned.1.call-done), kind=kOutput, calls=%fused_computation.18 | convolution fusion | flops 7521042432 | bytes 24903680 | tf_op jit(solution)/shard_map/enf,efd->end/dot_general | solution.py:183
  241.8 0.1 copy.69
  241.9 0.1 reshape.515
  242.0 0.4 copy-done.6
  242.4 0.1 copy.64
  242.6 0.2 select_reduce_fusion.1
  242.8 0.1 add.195
  243.0 0.1 select_reduce_fusion
  243.1 1.2 gather_fusion.1
  244.4 50.4 %reduce-scatter.6.cloned.1.call-done = bf16[1,32,4096]{2,1,0:T(8,128)(2,1)} async-done(((bf16[1,512,4096]{2,1,0:T(8,128)(2,1)}), bf16[1,32,4096]{2,1,0:T(8,128)(2,1)}) %reduce-scatter.6.cloned.1.call-update) | async-done | bytes 262160 | tf_op jit(solution)/shard_map/reduce_scatter | solution.py:182
  294.8 80.8 %reduce-scatter.8.cloned.1.call-done = bf16[1,32,4096]{2,1,0:T(8,128)(2,1)} async-done(((bf16[1,512,4096]{2,1,0:T(8,128)(2,1)}), bf16[1,32,4096]{2,1,0:T(8,128)(2,1)}) %reduce-scatter.8.cloned.1.call-update) | async-done | bytes 262160 | tf_op jit(solution)/shard_map/reduce_scatter | solution.py:182
  375.6 1.1 pad_maximum_fusion
  376.7 0.2 copy.78
  376.8 0.9 copy.80
  377.8 6.9 %all-to-all-start.1 = ((bf16[8,64,512]{2,1,0:T(8,128)(2,1)}), bf16[8,64,512]{2,1,0:T(8,128)(2,1)S(1)}, u32[]{:S(2)}, u32[]{:S(2)}) async-start(bf16[8,64,512]{2,1,0:T(8,128)(2,1)} %bitcast.126), calls=%async_computation.4 | async-start | bytes 1048576 | tf_op jit(solution)/shard_map/all_to_all | solution.py:194
  384.7 0.3 copy.70
  385.0 0.7 gather_fusion.2
  385.8 0.3 copy.71
  386.0 0.7 gather_fusion.3
  386.8 0.8 pad_maximum_fusion.2
  387.6 6.4 %all-to-all-done.1 = bf16[8,64,512]{2,1,0:T(8,128)(2,1)S(1)} async-done(((bf16[8,64,512]{2,1,0:T(8,128)(2,1)}), bf16[8,64,512]{2,1,0:T(8,128)(2,1)S(1)}, u32[]{:S(2)}, u32[]{:S(2)}) %all-to-all-start.1) | async-done | bytes 524320 | tf_op jit(solution)/shard_map/all_to_all | solution.py:194
  394.0 1.2 gather_fusion
  395.1 0.3 reshape.521
  395.5 0.7 multiply_reduce_fusion
  396.2 0.7 add_convert_fusion
  (52 shorter events, 0.9 us)
Async XLA Ops:
  7.2 48.4 %all-gather.4.cloned.1.call-start = ((), (), s32[]{:S(2)}) async-start(), calls=%async_computation.5 | async-start | bytes 1114112 | tf_op jit(solution)/shard_map/all_gather | solution.py:95
  10.8 82.5 %reduce-scatter.4.cloned.1.call-start = ((), (), s32[]{:S(2)}) async-start(), calls=%async_computation.6 | async-start | bytes 1179648 | tf_op jit(solution)/shard_map/reduce_scatter | solution.py:134
  55.5 3.0 copy-start.1
  58.6 2.2 copy-start
  59.6 2.9 copy-start.5
  59.6 33.6 %copy-start.2 = (bf16[128,512]{1,0:T(8,128)(2,1)S(1)}, bf16[128,512]{1,0:T(8,128)(2,1)}, u32[]{:S(2)}) copy-start(bf16[128,512]{1,0:T(8,128)(2,1)} %param.13) | copy-start | bytes 393220
  62.5 47.8 %copy-start.4 = (f32[4096]{0:T(1024)S(1)}, f32[4096]{0:T(1024)}, u32[]{:S(2)}) copy-start(f32[4096]{0:T(1024)} %param.20) | copy-start | bytes 49156
  62.5 99.6 %all-gather.6.cloned.1.call-start = ((), (), s32[]{:S(2)}) async-start(), calls=%async_computation.7 | async-start | bytes 4456448 | tf_op jit(solution)/shard_map/all_gather | solution.py:173
  111.3 103.8 %all-gather.8.cloned.1.call-start = ((), (), s32[]{:S(2)}) async-start(), calls=%async_computation.9 | async-start | bytes 4456448 | tf_op jit(solution)/shard_map/all_gather | solution.py:173
  111.9 182.9 %reduce-scatter.6.cloned.1.call-start = ((), (), s32[]{:S(2)}) async-start(), calls=%async_computation.8 | async-start | bytes 4456448 | tf_op jit(solution)/shard_map/reduce_scatter | solution.py:182
  188.8 186.7 %reduce-scatter.8.cloned.1.call-start = ((), (), s32[]{:S(2)}) async-start(), calls=%async_computation.10 | async-start | bytes 4456448 | tf_op jit(solution)/shard_map/reduce_scatter | solution.py:182
  241.7 0.7 copy-start.6
  241.7 0.8 copy-start.7
  241.7 1.2 copy-start.8
  377.8 16.2 %all-to-all-start.1 = ((bf16[8,64,512]{2,1,0:T(8,128)(2,1)}), bf16[8,64,512]{2,1,0:T(8,128)(2,1)S(1)}, u32[]{:S(2)}, u32[]{:S(2)}) async-start(bf16[8,64,512]{2,1,0:T(8,128)(2,1)} %bitcast.126), calls=%async_computation.4 | async-start | bytes 1048576 | tf_op jit(solution)/shard_map/all_to_all | solution.py:194
  384.6 11.6 %copy-start.3 = (bf16[128,512]{1,0:T(8,128)(2,1)S(1)}, bf16[128,512]{1,0:T(8,128)(2,1)}, u32[]{:S(2)}) copy-start(bf16[128,512]{1,0:T(8,128)(2,1)} %reduce-scatter.4.cloned.1.call-done) | copy-start | bytes 393220
Sparse Core Ops, SparseCore 0:
  10.9 44.5 all-gather.3
  62.6 30.5 reduce-scatter.3
  111.4 50.6 all-gather.5
  164.1 50.9 all-gather.7
  218.3 76.4 reduce-scatter.5
  298.0 77.5 reduce-scatter.7
